TPU v7x, 32 devices: a whole 2x2x4 slice. The times are simulated.
32 devices in a mesh: section: 2 (over x), fsdp: 16 (over z, y, core).
Axes of the slice: x: 2, y: 2, z: 4, core: 2. Of those that a mesh axis runs over, the one named last changes fastest.
Arguments:
- history: bfloat16 [4, 16, 32, 2048], P(None, 'fsdp'), may hold values from -6 to 6
- keymask: int32 [4, 16, 32], P(None, 'fsdp'), may hold values from 0 to 1, as said below
- codes: int32 [4, 16, 16, 2], P(None, 'fsdp'), may hold values from 0 to 15
- plan_table: bfloat16 [16, 2048], replicated, may hold values from -6 to 6
- query_weights: bfloat16 [2, 2048, 1024], P('section', 'fsdp'), may hold values from -0.125 to 0.125
- output_weights: bfloat16 [2, 1024, 2048], P('section', 'fsdp'), may hold values from -0.75 to 0.75
- gains: float32 [2, 2048], P('section'), may hold values from 0.5 to 1.5
- cotangent: bfloat16 [4, 16, 32, 2048], P(None, 'fsdp'), may hold values from -6 to 6
Outputs:
- section_grads: bfloat16 [2, 4, 16, 32, 2048], P('section', None, 'fsdp')
- gain_grads: float32 [2, 2048], P('section')
Inputs may be any that keep to these rules, and one draw needn't show every extreme that they name: `keymask`: in each series the ones form one run that ends at the last position and covers at least a quarter of the 32 positions.
All inputs are finite; a program needn't handle non-finite values.
Results may differ from a plain program's by a relative error of at most 0.014.
Values may be sent and summed in bfloat16 or wider, within the bound.
No kernel may reach another device: no remote copies, remote signals or barrier semaphores. Data moves between devices by JAX's collectives and lax.ppermute only.
A program may use at most 64 MiB of HBM per device.

v0:
```python
import math
import jax
import jax.numpy as jnp
from jax import lax
from jax.sharding import PartitionSpec as P

HEADS = 8
EPSILON = 1e-05


def shifted(array, axis, by):
    size = lax.axis_size(axis)
    pairs = [(i, i + by) for i in range(size) if 0 <= i + by < size]
    return lax.ppermute(array, axis, pairs)


def rms_scale(inputs, gain_vector):
    return (
        inputs
        * lax.rsqrt(jnp.mean(inputs * inputs, axis=-1, keepdims=True) + EPSILON)
        * gain_vector
    )


def attend_layer(section_input, source, key_mask, query_weight, output_weight, gain_vector):
    series_count, seq_length, model_width = section_input.shape
    half_width = model_width // 2
    head_dim = half_width // HEADS
    head_shape = (series_count, seq_length, HEADS, head_dim)
    input_wide = section_input.astype(jnp.float32)
    normed = rms_scale(input_wide, gain_vector)
    normed_source = rms_scale(source.astype(jnp.float32), gain_vector)
    normed_rows = normed.astype(jnp.bfloat16).reshape(series_count * seq_length, model_width)
    query_flat = jnp.dot(normed_rows, query_weight, preferred_element_type=jnp.float32)
    queries = query_flat.astype(jnp.bfloat16).reshape(head_shape)
    key_rows = normed_source[..., :half_width].astype(jnp.bfloat16).reshape(head_shape)
    value_rows = normed_source[..., half_width:].astype(jnp.bfloat16).reshape(head_shape)
    scores = jnp.einsum(
        "bqhd,bkhd->bhqk", queries, key_rows, preferred_element_type=jnp.float32
    ) / math.sqrt(head_dim)
    raised = jnp.exp(scores) * key_mask.astype(jnp.float32)[:, None, None, :]
    probs = (raised / jnp.sum(raised, axis=-1, keepdims=True)).astype(jnp.bfloat16)
    mixed = jnp.einsum("bhqk,bkhd->bqhd", probs, value_rows, preferred_element_type=jnp.float32)
    mixed = mixed.astype(jnp.bfloat16).reshape(series_count * seq_length, half_width)
    update = jnp.dot(mixed, output_weight, preferred_element_type=jnp.float32)
    return (input_wide + update.reshape(series_count, seq_length, model_width)).astype(jnp.bfloat16)


def pick_slot(stack, slot):
    return lax.dynamic_index_in_dim(stack, slot, 0, False)


def place_slot(stack, slot, update, keep):
    previous = pick_slot(stack, slot)
    return lax.dynamic_update_index_in_dim(stack, jnp.where(keep, update, previous), slot, 0)


def on_device(history, keymask, codes, plan_table, query_weights, output_weights, gains, cotangent):
    section_index = lax.axis_index("section")
    section_count = lax.axis_size("section")
    half_sections = section_count // 2
    micro_count, series_count, seq_length, model_width = history.shape
    gathered_query, gathered_output = (
        lax.all_gather(query_weights, "fsdp", axis=1, tiled=True),
        lax.all_gather(output_weights, "fsdp", axis=1, tiled=True),
    )
    query_weight = gathered_query[0]
    output_weight = gathered_output[0]
    gain_vector = gains[0]
    code_rows = codes.reshape(micro_count, series_count, seq_length)
    code_count = plan_table.shape[0]
    one_hot = (code_rows[..., None] == jnp.arange(code_count, dtype=jnp.int32)).astype(jnp.bfloat16)
    plan_tokens = jnp.einsum(
        "msln,nd->msld", one_hot, plan_table, preferred_element_type=jnp.float32
    ).astype(jnp.bfloat16)
    is_decoder = section_index >= half_sections
    zero_act = jnp.zeros((series_count, seq_length, model_width), jnp.bfloat16)
    zero_stack = jnp.zeros(history.shape, jnp.bfloat16)
    tick_count = micro_count + section_count - 1

    def forward_tick(tick_index, state_tuple):
        got_input, got_memory, inputs_buf, memory_buf = state_tuple
        micro_index = tick_index - section_index
        is_active = (micro_index >= 0) & (micro_index < micro_count)
        slot = jnp.clip(micro_index, 0, micro_count - 1)
        key_mask = pick_slot(keymask, slot)
        section_input = jnp.where(
            section_index == 0,
            pick_slot(history, slot),
            jnp.where(section_index == half_sections, pick_slot(plan_tokens, slot), got_input),
        )
        memory = got_memory
        source = jnp.where(is_decoder, memory, section_input)

        def run_layer():
            return attend_layer(
                section_input, source, key_mask, query_weight, output_weight, gain_vector
            )

        def skip_layer():
            return zero_act

        output = lax.cond(is_active, run_layer, skip_layer)
        inputs_buf = place_slot(inputs_buf, slot, section_input, is_active)
        memory_buf = place_slot(memory_buf, slot, memory, is_active & is_decoder)
        outgoing = jnp.where(
            section_index == half_sections - 1, output, jnp.where(is_decoder, memory, zero_act)
        )
        got_input, got_memory = shifted((output, outgoing), "section", 1)
        return (got_input, got_memory, inputs_buf, memory_buf)

    start_state = (zero_act, zero_act, zero_stack, zero_stack)
    _, _, inputs_buf, memory_buf = lax.fori_loop(0, tick_count, forward_tick, start_state)

    def backward_tick(tick_index, state_tuple):
        got_grad, got_memory_grad, grads_buf, gain_total = state_tuple
        micro_index = tick_index - (section_count - 1 - section_index)
        is_active = (micro_index >= 0) & (micro_index < micro_count)
        slot = jnp.clip(micro_index, 0, micro_count - 1)
        key_mask = pick_slot(keymask, slot)
        out_grad = jnp.where(
            section_index == section_count - 1, pick_slot(cotangent, slot), got_grad
        )
        section_input = pick_slot(inputs_buf, slot)
        memory = pick_slot(memory_buf, slot)

        def section_map(layer_input, layer_memory, layer_gain):
            layer_source = jnp.where(is_decoder, layer_memory, layer_input)
            return attend_layer(
                layer_input, layer_source, key_mask, query_weight, output_weight, layer_gain
            )

        def run_grads():
            _, pull = jax.vjp(section_map, section_input, memory, gain_vector)
            return pull(out_grad)

        def skip_grads():
            return (zero_act, zero_act, jnp.zeros_like(gain_vector))

        input_grad, memory_grad, gain_grad = lax.cond(is_active, run_grads, skip_grads)
        memory_sum = jnp.where(is_decoder, got_memory_grad + memory_grad, zero_act)
        send_main = jnp.where(section_index == half_sections, memory_sum, input_grad)
        send_side = jnp.where(is_decoder & (section_index != half_sections), memory_sum, zero_act)
        got_grad, got_memory_grad = shifted((send_main, send_side), "section", -1)
        grads_buf = place_slot(grads_buf, slot, input_grad, is_active)
        gain_total = gain_total + lax.psum(gain_grad, "fsdp")
        return (got_grad, got_memory_grad, grads_buf, gain_total)

    back_state = (zero_act, zero_act, zero_stack, jnp.zeros_like(gain_vector))
    _, _, grads_buf, gain_total = lax.fori_loop(0, tick_count, backward_tick, back_state)
    return (grads_buf[None], gain_total[None])


def solution(mesh):
    return jax.shard_map(
        on_device,
        mesh=mesh,
        in_specs=(
            P(None, "fsdp", None, None),
            P(None, "fsdp", None),
            P(None, "fsdp", None, None),
            P(),
            P("section", "fsdp", None),
            P("section", "fsdp", None),
            P("section", None),
            P(None, "fsdp", None, None),
        ),
        out_specs=(P("section", None, "fsdp", None, None), P("section", None)),
        check_vma=False,
    )
```

profile of v0, /device:TPU:0, one launch (start us, length us, event | category | flops | bytes accessed | tf_op | source)
XLA Modules:
  0.0 415.8 jit_solution(3246150808287306456)
XLA Ops:
  9.9 53.6 %all-gather.3.cloned.1.call-done = bf16[1,1024,2048]{2,1,0:T(8,128)(2,1)} async-done(((bf16[1,64,2048]{2,1,0:T(8,128)(2,1)}), bf16[1,1024,2048]{2,1,0:T(8,128)(2,1)}) %all-gather.3.cloned.1.call-update) | async-done | bytes 4194320 | tf_op jit(solution)/shard_map/all_gather | solution.py:65
  63.5 51.2 %all-gather.5.cloned.1.call-done = bf16[1,2048,1024]{2,1,0:T(8,128)(2,1)} async-done(((bf16[1,128,1024]{2,1,0:T(8,128)(2,1)}), bf16[1,2048,1024]{2,1,0:T(8,128)(2,1)}) %all-gather.5.cloned.1.call-update) | async-done | bytes 4194320 | tf_op jit(solution)/shard_map/all_gather | solution.py:64
  114.9 89.8 %while.42 = (s32[]{:T(128)}, bf16[1,32,2048]{2,1,0:T(8,128)(2,1)S(1)}, bf16[1,32,2048]{2,1,0:T(8,128)(2,1)S(1)}, bf16[4,1,32,2048]{3,2,1,0:T(8,128)(2,1)S(1)}, b...) while((s32[]{:T(128)}, ...), condition=%wide.region_6.7_spmd, body=%wide.region_0.6_spmd.sunk | while | flops 274366848 | bytes 14173985 | solution.py:113
  114.9 1.0 bitcast_dynamic-update-slice_fusion.6
  116.0 8.3 %conditional.5 = (bf16[1,32,2048]{2,1,0:T(8,128)(2,1)S(1)}) conditional(s32[]{:T(128)} %convert_element_type.398, () %tuple.120, (bf16[1,32,2048]{2,1,0:T(8,128)(2,1)S(1)}, pred[1,32,2048]{2,1,0:T(8,128)(4,1)S(1)}, bf16[1,32,2048]{2,1,0:T(8,128)(2,1)S(1)}, f32[1,2048]{1,0:T(1,128)}, bf16[2048,1024]{1,0:T(8,128)(2,1)}, ...), branch_computations={%region_1.1_spmd, %region_2.5_spmd} | conditional | flops 273973632 | bytes 10700172 | solution.py:103
  117.0 3.1 fusion.5
  121.2 3.0 fusion.1
  124.3 1.3 collective-permute-start
  125.6 1.3 collective-permute-start.1
  127.0 4.8 %collective-permute-done.1 = bf16[1,32,2048]{2,1,0:T(8,128)(2,1)S(1)} collective-permute-done((bf16[1,32,2048]{2,1,0:T(8,128)(2,1)S(1)}, bf16[1,32,2048]{2,1,0:T(8,128)(2,1)S(1)}, u32[]{:S(2)}, u32[]{:S(2)}) %collective-permute-start.1) | collective-permute-done | bytes 131104 | tf_op jit(solution)/shard_map/while/body/eval_jaxpr/ppermute | solution.py:14
  132.9 8.3 %conditional.5 = (bf16[1,32,2048]{2,1,0:T(8,128)(2,1)S(1)}) conditional(s32[]{:T(128)} %convert_element_type.398, () %tuple.120, (bf16[1,32,2048]{2,1,0:T(8,128)(2,1)S(1)}, pred[1,32,2048]{2,1,0:T(8,128)(4,1)S(1)}, bf16[1,32,2048]{2,1,0:T(8,128)(2,1)S(1)}, f32[1,2048]{1,0:T(1,128)}, bf16[2048,1024]{1,0:T(8,128)(2,1)}, ...), branch_computations={%region_1.1_spmd, %region_2.5_spmd} | conditional | flops 273973632 | bytes 10700172 | solution.py:103
  134.0 3.1 fusion.5
  138.2 3.0 fusion.1
  141.2 4.4 %collective-permute-start = (bf16[1,32,2048]{2,1,0:T(8,128)(2,1)S(1)}, bf16[1,32,2048]{2,1,0:T(8,128)(2,1)S(1)}, u32[]{:S(2)}, u32[]{:S(2)}) collective-permute-start(bf16[1,32,2048]{2,1,0:T(8,128)(2,1)S(1)} %get-tuple-element.1286), channel_id=1, source_target_pairs={{0,16},{1,17},{2,18},{3,19},{4,20},{5,21},{6,22},{7,23},{8,24},{9,... | collective-permute-start | bytes 393224 | tf_op jit(solution)/shard_map/while/body/eval_jaxpr/ppermute | solution.py:14
  145.6 1.3 collective-permute-start.1
  147.0 4.0 collective-permute-done.1
  151.1 1.0 bitcast_dynamic-update-slice_fusion.6
  152.1 8.3 %conditional.5 = (bf16[1,32,2048]{2,1,0:T(8,128)(2,1)S(1)}) conditional(s32[]{:T(128)} %convert_element_type.398, () %tuple.120, (bf16[1,32,2048]{2,1,0:T(8,128)(2,1)S(1)}, pred[1,32,2048]{2,1,0:T(8,128)(4,1)S(1)}, bf16[1,32,2048]{2,1,0:T(8,128)(2,1)S(1)}, f32[1,2048]{1,0:T(1,128)}, bf16[2048,1024]{1,0:T(8,128)(2,1)}, ...), branch_computations={%region_1.1_spmd, %region_2.5_spmd} | conditional | flops 273973632 | bytes 10700172 | solution.py:103
  153.2 3.1 fusion.5
  157.4 3.0 fusion.1
  160.4 4.4 %collective-permute-start = (bf16[1,32,2048]{2,1,0:T(8,128)(2,1)S(1)}, bf16[1,32,2048]{2,1,0:T(8,128)(2,1)S(1)}, u32[]{:S(2)}, u32[]{:S(2)}) collective-permute-start(bf16[1,32,2048]{2,1,0:T(8,128)(2,1)S(1)} %get-tuple-element.1286), channel_id=1, source_target_pairs={{0,16},{1,17},{2,18},{3,19},{4,20},{5,21},{6,22},{7,23},{8,24},{9,... | collective-permute-start | bytes 393224 | tf_op jit(solution)/shard_map/while/body/eval_jaxpr/ppermute | solution.py:14
  164.8 1.3 collective-permute-start.1
  166.2 3.2 collective-permute-done.1
  170.5 8.3 %conditional.5 = (bf16[1,32,2048]{2,1,0:T(8,128)(2,1)S(1)}) conditional(s32[]{:T(128)} %convert_element_type.398, () %tuple.120, (bf16[1,32,2048]{2,1,0:T(8,128)(2,1)S(1)}, pred[1,32,2048]{2,1,0:T(8,128)(4,1)S(1)}, bf16[1,32,2048]{2,1,0:T(8,128)(2,1)S(1)}, f32[1,2048]{1,0:T(1,128)}, bf16[2048,1024]{1,0:T(8,128)(2,1)}, ...), branch_computations={%region_1.1_spmd, %region_2.5_spmd} | conditional | flops 273973632 | bytes 10700172 | solution.py:103
  171.5 3.1 fusion.5
  175.7 3.0 fusion.1
  178.8 4.4 %collective-permute-start = (bf16[1,32,2048]{2,1,0:T(8,128)(2,1)S(1)}, bf16[1,32,2048]{2,1,0:T(8,128)(2,1)S(1)}, u32[]{:S(2)}, u32[]{:S(2)}) collective-permute-start(bf16[1,32,2048]{2,1,0:T(8,128)(2,1)S(1)} %get-tuple-element.1286), channel_id=1, source_target_pairs={{0,16},{1,17},{2,18},{3,19},{4,20},{5,21},{6,22},{7,23},{8,24},{9,... | collective-permute-start | bytes 393224 | tf_op jit(solution)/shard_map/while/body/eval_jaxpr/ppermute | solution.py:14
  183.2 1.3 collective-permute-start.1
  184.6 2.5 collective-permute-done.1
  188.2 12.6 %collective-permute-start = (bf16[1,32,2048]{2,1,0:T(8,128)(2,1)S(1)}, bf16[1,32,2048]{2,1,0:T(8,128)(2,1)S(1)}, u32[]{:S(2)}, u32[]{:S(2)}) collective-permute-start(bf16[1,32,2048]{2,1,0:T(8,128)(2,1)S(1)} %get-tuple-element.1286), channel_id=1, source_target_pairs={{0,16},{1,17},{2,18},{3,19},{4,20},{5,21},{6,22},{7,23},{8,24},{9,... | collective-permute-start | bytes 393224 | tf_op jit(solution)/shard_map/while/body/eval_jaxpr/ppermute | solution.py:14
  200.8 1.3 collective-permute-start.1
  202.2 2.5 collective-permute-done.1
  204.8 203.3 %while.43 = (s32[]{:T(128)}, bf16[1,32,2048]{2,1,0:T(8,128)(2,1)S(1)}, bf16[1,32,2048]{2,1,0:T(8,128)(2,1)S(1)}, bf16[4,1,32,2048]{3,2,1,0:T(8,128)(2,1)S(1)}, f...) while((s32[]{:T(128)}, ...), condition=%wide.region_19.20_spmd.clone, body=%wide.region_7.19_spmd.clone.sunk | while | flops 417616544 | bytes 54182452 | solution.py:150
  205.0 1.3 collective-permute-start.2
  206.3 1.3 collective-permute-start.3
  207.6 30.0 %psum.15 = f32[2048]{0:T(1024)S(1)} all-reduce(f32[2048]{0:T(1024)S(1)} %get-tuple-element.1162), channel_id=1, replica_groups=mesh['section'=2,'fsdp'=16] {'fsdp'}, use_global_device_ids=true, to_apply=%region_18.18 | all-reduce | flops 2048 | bytes 16384 | tf_op jit(solution)/shard_map/while/body/eval_jaxpr/psum | solution.py:146
  237.8 9.8 %conditional.6 = (bf16[1,32,2048]{2,1,0:T(8,128)(2,1)S(1)}, bf16[1,32,2048]{2,1,0:T(8,128)(2,1)S(1)}, f32[2048]{0:T(1024)S(1)}) conditional(s32[]{:T(128)} %convert_element_type.399, () %tuple.124, (bf16[4,1,32,2048]{3,2,1,0:T(8,128)(2,1)S(1)}, s32[]{:T(128)}, pred[1,32,2048]{2,1,0:T(32,128)(4,1)S(1)}, bf16[1,32,2048]{2,1,0:T(8,128)(2,1)S(1)}, ...), branch_computations={%region_8.8_spmd, %region_9.17_spmd} | conditional | flops 417282720 | bytes 51716228 | solution.py:140
  239.0 3.1 fusion.38
  243.2 1.3 fusion.37
  245.7 1.5 fusion.50
  247.6 1.3 collective-permute-start.2
  248.9 1.3 collective-permute-start.3
  250.3 30.0 %psum.15 = f32[2048]{0:T(1024)S(1)} all-reduce(f32[2048]{0:T(1024)S(1)} %get-tuple-element.1162), channel_id=1, replica_groups=mesh['section'=2,'fsdp'=16] {'fsdp'}, use_global_device_ids=true, to_apply=%region_18.18 | all-reduce | flops 2048 | bytes 16384 | tf_op jit(solution)/shard_map/while/body/eval_jaxpr/psum | solution.py:146
  280.4 9.8 %conditional.6 = (bf16[1,32,2048]{2,1,0:T(8,128)(2,1)S(1)}, bf16[1,32,2048]{2,1,0:T(8,128)(2,1)S(1)}, f32[2048]{0:T(1024)S(1)}) conditional(s32[]{:T(128)} %convert_element_type.399, () %tuple.124, (bf16[4,1,32,2048]{3,2,1,0:T(8,128)(2,1)S(1)}, s32[]{:T(128)}, pred[1,32,2048]{2,1,0:T(32,128)(4,1)S(1)}, bf16[1,32,2048]{2,1,0:T(8,128)(2,1)S(1)}, ...), branch_computations={%region_8.8_spmd, %region_9.17_spmd} | conditional | flops 417282720 | bytes 51716228 | solution.py:140
  281.6 3.1 fusion.38
  285.8 1.3 fusion.37
  288.4 1.5 fusion.50
  290.2 1.3 collective-permute-start.2
  291.5 1.3 collective-permute-start.3
  292.9 30.0 %psum.15 = f32[2048]{0:T(1024)S(1)} all-reduce(f32[2048]{0:T(1024)S(1)} %get-tuple-element.1162), channel_id=1, replica_groups=mesh['section'=2,'fsdp'=16] {'fsdp'}, use_global_device_ids=true, to_apply=%region_18.18 | all-reduce | flops 2048 | bytes 16384 | tf_op jit(solution)/shard_map/while/body/eval_jaxpr/psum | solution.py:146
  323.0 9.8 %conditional.6 = (bf16[1,32,2048]{2,1,0:T(8,128)(2,1)S(1)}, bf16[1,32,2048]{2,1,0:T(8,128)(2,1)S(1)}, f32[2048]{0:T(1024)S(1)}) conditional(s32[]{:T(128)} %convert_element_type.399, () %tuple.124, (bf16[4,1,32,2048]{3,2,1,0:T(8,128)(2,1)S(1)}, s32[]{:T(128)}, pred[1,32,2048]{2,1,0:T(32,128)(4,1)S(1)}, bf16[1,32,2048]{2,1,0:T(8,128)(2,1)S(1)}, ...), branch_computations={%region_8.8_spmd, %region_9.17_spmd} | conditional | flops 417282720 | bytes 51716228 | solution.py:140
  324.2 3.1 fusion.38
  328.4 1.3 fusion.37
  331.0 1.5 fusion.50
  332.8 1.3 collective-permute-start.2
  334.1 1.3 collective-permute-start.3
  335.5 30.0 %psum.15 = f32[2048]{0:T(1024)S(1)} all-reduce(f32[2048]{0:T(1024)S(1)} %get-tuple-element.1162), channel_id=1, replica_groups=mesh['section'=2,'fsdp'=16] {'fsdp'}, use_global_device_ids=true, to_apply=%region_18.18 | all-reduce | flops 2048 | bytes 16384 | tf_op jit(solution)/shard_map/while/body/eval_jaxpr/psum | solution.py:146
  365.6 9.8 %conditional.6 = (bf16[1,32,2048]{2,1,0:T(8,128)(2,1)S(1)}, bf16[1,32,2048]{2,1,0:T(8,128)(2,1)S(1)}, f32[2048]{0:T(1024)S(1)}) conditional(s32[]{:T(128)} %convert_element_type.399, () %tuple.124, (bf16[4,1,32,2048]{3,2,1,0:T(8,128)(2,1)S(1)}, s32[]{:T(128)}, pred[1,32,2048]{2,1,0:T(32,128)(4,1)S(1)}, bf16[1,32,2048]{2,1,0:T(8,128)(2,1)S(1)}, ...), branch_computations={%region_8.8_spmd, %region_9.17_spmd} | conditional | flops 417282720 | bytes 51716228 | solution.py:140
  366.8 3.1 fusion.38
  371.0 1.3 fusion.37
  373.6 1.5 fusion.50
  375.4 1.3 collective-permute-start.2
  376.7 1.3 collective-permute-start.3
  378.1 30.0 %psum.15 = f32[2048]{0:T(1024)S(1)} all-reduce(f32[2048]{0:T(1024)S(1)} %get-tuple-element.1162), channel_id=1, replica_groups=mesh['section'=2,'fsdp'=16] {'fsdp'}, use_global_device_ids=true, to_apply=%region_18.18 | all-reduce | flops 2048 | bytes 16384 | tf_op jit(solution)/shard_map/while/body/eval_jaxpr/psum | solution.py:146
  (262 shorter events, 31.0 us)
Async XLA Ops:
  7.2 2.4 copy-start
  7.2 56.3 %all-gather.3.cloned.1.call-start = ((), (), s32[]{:S(2)}) async-start(), calls=%async_computation | async-start | bytes 4456448 | tf_op jit(solution)/shard_map/all_gather | solution.py:65
  7.9 106.8 %all-gather.5.cloned.1.call-start = ((), (), s32[]{:S(2)}) async-start(), calls=%async_computation.1 | async-start | bytes 4456448 | tf_op jit(solution)/shard_map/all_gather | solution.py:64
  114.9 89.9 %copy-start.4 = (bf16[4,1,32,2048]{3,2,1,0:T(8,128)(2,1)S(1)}, bf16[4,1,32,2048]{3,2,1,0:T(8,128)(2,1)}, u32[]{:S(2)}) copy-start(bf16[4,1,32,2048]{3,2,1,0:T(8,128)(2,1)} %param.23) | copy-start | bytes 1572868
  124.3 7.6 %collective-permute-start = (bf16[1,32,2048]{2,1,0:T(8,128)(2,1)S(1)}, bf16[1,32,2048]{2,1,0:T(8,128)(2,1)S(1)}, u32[]{:S(2)}, u32[]{:S(2)}) collective-permute-start(bf16[1,32,2048]{2,1,0:T(8,128)(2,1)S(1)} %get-tuple-element.1286), channel_id=1, source_target_pairs={{0,16},{1,17},{2,18},{3,19},{4,20},{5,21},{6,22},{7,23},{8,24},{9,... | collective-permute-start | bytes 393224 | tf_op jit(solution)/shard_map/while/body/eval_jaxpr/ppermute | solution.py:14
  125.6 6.2 %collective-permute-start.1 = (bf16[1,32,2048]{2,1,0:T(8,128)(2,1)S(1)}, bf16[1,32,2048]{2,1,0:T(8,128)(2,1)S(1)}, u32[]{:S(2)}, u32[]{:S(2)}) collective-permute-start(bf16[1,32,2048]{2,1,0:T(8,128)(2,1)S(1)} %select_select_fusion.2), channel_id=1, source_target_pairs={{0,16},{1,17},{2,18},{3,19},{4,20},{5,21},{6,22},{7,23},{8,24},{9,... | collective-permute-start | bytes 393224 | tf_op jit(solution)/shard_map/while/body/eval_jaxpr/ppermute | solution.py:14
  141.2 9.9 %collective-permute-start = (bf16[1,32,2048]{2,1,0:T(8,128)(2,1)S(1)}, bf16[1,32,2048]{2,1,0:T(8,128)(2,1)S(1)}, u32[]{:S(2)}, u32[]{:S(2)}) collective-permute-start(bf16[1,32,2048]{2,1,0:T(8,128)(2,1)S(1)} %get-tuple-element.1286), channel_id=1, source_target_pairs={{0,16},{1,17},{2,18},{3,19},{4,20},{5,21},{6,22},{7,23},{8,24},{9,... | collective-permute-start | bytes 393224 | tf_op jit(solution)/shard_map/while/body/eval_jaxpr/ppermute | solution.py:14
  145.6 5.4 %collective-permute-start.1 = (bf16[1,32,2048]{2,1,0:T(8,128)(2,1)S(1)}, bf16[1,32,2048]{2,1,0:T(8,128)(2,1)S(1)}, u32[]{:S(2)}, u32[]{:S(2)}) collective-permute-start(bf16[1,32,2048]{2,1,0:T(8,128)(2,1)S(1)} %select_select_fusion.2), channel_id=1, source_target_pairs={{0,16},{1,17},{2,18},{3,19},{4,20},{5,21},{6,22},{7,23},{8,24},{9,... | collective-permute-start | bytes 393224 | tf_op jit(solution)/shard_map/while/body/eval_jaxpr/ppermute | solution.py:14
  160.4 9.0 %collective-permute-start = (bf16[1,32,2048]{2,1,0:T(8,128)(2,1)S(1)}, bf16[1,32,2048]{2,1,0:T(8,128)(2,1)S(1)}, u32[]{:S(2)}, u32[]{:S(2)}) collective-permute-start(bf16[1,32,2048]{2,1,0:T(8,128)(2,1)S(1)} %get-tuple-element.1286), channel_id=1, source_target_pairs={{0,16},{1,17},{2,18},{3,19},{4,20},{5,21},{6,22},{7,23},{8,24},{9,... | collective-permute-start | bytes 393224 | tf_op jit(solution)/shard_map/while/body/eval_jaxpr/ppermute | solution.py:14
  164.8 4.5 %collective-permute-start.1 = (bf16[1,32,2048]{2,1,0:T(8,128)(2,1)S(1)}, bf16[1,32,2048]{2,1,0:T(8,128)(2,1)S(1)}, u32[]{:S(2)}, u32[]{:S(2)}) collective-permute-start(bf16[1,32,2048]{2,1,0:T(8,128)(2,1)S(1)} %select_select_fusion.2), channel_id=1, source_target_pairs={{0,16},{1,17},{2,18},{3,19},{4,20},{5,21},{6,22},{7,23},{8,24},{9,... | collective-permute-start | bytes 393224 | tf_op jit(solution)/shard_map/while/body/eval_jaxpr/ppermute | solution.py:14
  178.8 8.3 %collective-permute-start = (bf16[1,32,2048]{2,1,0:T(8,128)(2,1)S(1)}, bf16[1,32,2048]{2,1,0:T(8,128)(2,1)S(1)}, u32[]{:S(2)}, u32[]{:S(2)}) collective-permute-start(bf16[1,32,2048]{2,1,0:T(8,128)(2,1)S(1)} %get-tuple-element.1286), channel_id=1, source_target_pairs={{0,16},{1,17},{2,18},{3,19},{4,20},{5,21},{6,22},{7,23},{8,24},{9,... | collective-permute-start | bytes 393224 | tf_op jit(solution)/shard_map/while/body/eval_jaxpr/ppermute | solution.py:14
  183.2 3.8 collective-permute-start.1
  188.2 16.5 %collective-permute-start = (bf16[1,32,2048]{2,1,0:T(8,128)(2,1)S(1)}, bf16[1,32,2048]{2,1,0:T(8,128)(2,1)S(1)}, u32[]{:S(2)}, u32[]{:S(2)}) collective-permute-start(bf16[1,32,2048]{2,1,0:T(8,128)(2,1)S(1)} %get-tuple-element.1286), channel_id=1, source_target_pairs={{0,16},{1,17},{2,18},{3,19},{4,20},{5,21},{6,22},{7,23},{8,24},{9,... | collective-permute-start | bytes 393224 | tf_op jit(solution)/shard_map/while/body/eval_jaxpr/ppermute | solution.py:14
  200.8 3.8 collective-permute-start.1
  205.0 32.7 %collective-permute-start.2 = (bf16[1,32,2048]{2,1,0:T(8,128)(2,1)S(1)}, bf16[1,32,2048]{2,1,0:T(8,128)(2,1)S(1)}, u32[]{:S(2)}, u32[]{:S(2)}) collective-permute-start(bf16[1,32,2048]{2,1,0:T(8,128)(2,1)S(1)} %get-tuple-element.1160), channel_id=1, source_target_pairs={{16,0},{17,1},{18,2},{19,3},{20,4},{21,5},{22,6},{23,7},{24,8},{25... | collective-permute-start | bytes 393224 | tf_op jit(solution)/shard_map/while/body/eval_jaxpr/ppermute | solution.py:14
  206.3 31.4 %collective-permute-start.3 = (bf16[1,32,2048]{2,1,0:T(8,128)(2,1)S(1)}, bf16[1,32,2048]{2,1,0:T(8,128)(2,1)S(1)}, u32[]{:S(2)}, u32[]{:S(2)}) collective-permute-start(bf16[1,32,2048]{2,1,0:T(8,128)(2,1)S(1)} %get-tuple-element.1161), channel_id=1, source_target_pairs={{16,0},{17,1},{18,2},{19,3},{20,4},{21,5},{22,6},{23,7},{24,8},{25... | collective-permute-start | bytes 393224 | tf_op jit(solution)/shard_map/while/body/eval_jaxpr/ppermute | solution.py:14
  237.8 5.4 %copy-start.2 = (bf16[1024,2048]{1,0:T(8,128)(2,1)S(1)}, bf16[1024,2048]{1,0:T(8,128)(2,1)}, u32[]{:S(2)}) copy-start(bf16[1024,2048]{1,0:T(8,128)(2,1)} %get-tuple-element.750) | copy-start | bytes 12582916 | tf_op jit(solution)/shard_map/while/body/eval_jaxpr/cond
  242.1 3.1 copy-start.3
  242.1 3.6 copy-start.1
  247.6 32.7 %collective-permute-start.2 = (bf16[1,32,2048]{2,1,0:T(8,128)(2,1)S(1)}, bf16[1,32,2048]{2,1,0:T(8,128)(2,1)S(1)}, u32[]{:S(2)}, u32[]{:S(2)}) collective-permute-start(bf16[1,32,2048]{2,1,0:T(8,128)(2,1)S(1)} %get-tuple-element.1160), channel_id=1, source_target_pairs={{16,0},{17,1},{18,2},{19,3},{20,4},{21,5},{22,6},{23,7},{24,8},{25... | collective-permute-start | bytes 393224 | tf_op jit(solution)/shard_map/while/body/eval_jaxpr/ppermute | solution.py:14
  248.9 31.4 %collective-permute-start.3 = (bf16[1,32,2048]{2,1,0:T(8,128)(2,1)S(1)}, bf16[1,32,2048]{2,1,0:T(8,128)(2,1)S(1)}, u32[]{:S(2)}, u32[]{:S(2)}) collective-permute-start(bf16[1,32,2048]{2,1,0:T(8,128)(2,1)S(1)} %get-tuple-element.1161), channel_id=1, source_target_pairs={{16,0},{17,1},{18,2},{19,3},{20,4},{21,5},{22,6},{23,7},{24,8},{25... | collective-permute-start | bytes 393224 | tf_op jit(solution)/shard_map/while/body/eval_jaxpr/ppermute | solution.py:14
  280.4 5.4 %copy-start.2 = (bf16[1024,2048]{1,0:T(8,128)(2,1)S(1)}, bf16[1024,2048]{1,0:T(8,128)(2,1)}, u32[]{:S(2)}) copy-start(bf16[1024,2048]{1,0:T(8,128)(2,1)} %get-tuple-element.750) | copy-start | bytes 12582916 | tf_op jit(solution)/shard_map/while/body/eval_jaxpr/cond
  284.7 3.1 copy-start.3
  284.8 3.6 copy-start.1
  290.2 32.7 %collective-permute-start.2 = (bf16[1,32,2048]{2,1,0:T(8,128)(2,1)S(1)}, bf16[1,32,2048]{2,1,0:T(8,128)(2,1)S(1)}, u32[]{:S(2)}, u32[]{:S(2)}) collective-permute-start(bf16[1,32,2048]{2,1,0:T(8,128)(2,1)S(1)} %get-tuple-element.1160), channel_id=1, source_target_pairs={{16,0},{17,1},{18,2},{19,3},{20,4},{21,5},{22,6},{23,7},{24,8},{25... | collective-permute-start | bytes 393224 | tf_op jit(solution)/shard_map/while/body/eval_jaxpr/ppermute | solution.py:14
  291.5 31.4 %collective-permute-start.3 = (bf16[1,32,2048]{2,1,0:T(8,128)(2,1)S(1)}, bf16[1,32,2048]{2,1,0:T(8,128)(2,1)S(1)}, u32[]{:S(2)}, u32[]{:S(2)}) collective-permute-start(bf16[1,32,2048]{2,1,0:T(8,128)(2,1)S(1)} %get-tuple-element.1161), channel_id=1, source_target_pairs={{16,0},{17,1},{18,2},{19,3},{20,4},{21,5},{22,6},{23,7},{24,8},{25... | collective-permute-start | bytes 393224 | tf_op jit(solution)/shard_map/while/body/eval_jaxpr/ppermute | solution.py:14
  323.0 5.4 %copy-start.2 = (bf16[1024,2048]{1,0:T(8,128)(2,1)S(1)}, bf16[1024,2048]{1,0:T(8,128)(2,1)}, u32[]{:S(2)}) copy-start(bf16[1024,2048]{1,0:T(8,128)(2,1)} %get-tuple-element.750) | copy-start | bytes 12582916 | tf_op jit(solution)/shard_map/while/body/eval_jaxpr/cond
  327.4 3.1 copy-start.3
  327.4 3.6 copy-start.1
  332.8 32.7 %collective-permute-start.2 = (bf16[1,32,2048]{2,1,0:T(8,128)(2,1)S(1)}, bf16[1,32,2048]{2,1,0:T(8,128)(2,1)S(1)}, u32[]{:S(2)}, u32[]{:S(2)}) collective-permute-start(bf16[1,32,2048]{2,1,0:T(8,128)(2,1)S(1)} %get-tuple-element.1160), channel_id=1, source_target_pairs={{16,0},{17,1},{18,2},{19,3},{20,4},{21,5},{22,6},{23,7},{24,8},{25... | collective-permute-start | bytes 393224 | tf_op jit(solution)/shard_map/while/body/eval_jaxpr/ppermute | solution.py:14
  334.1 31.4 %collective-permute-start.3 = (bf16[1,32,2048]{2,1,0:T(8,128)(2,1)S(1)}, bf16[1,32,2048]{2,1,0:T(8,128)(2,1)S(1)}, u32[]{:S(2)}, u32[]{:S(2)}) collective-permute-start(bf16[1,32,2048]{2,1,0:T(8,128)(2,1)S(1)} %get-tuple-element.1161), channel_id=1, source_target_pairs={{16,0},{17,1},{18,2},{19,3},{20,4},{21,5},{22,6},{23,7},{24,8},{25... | collective-permute-start | bytes 393224 | tf_op jit(solution)/shard_map/while/body/eval_jaxpr/ppermute | solution.py:14
  365.6 5.4 %copy-start.2 = (bf16[1024,2048]{1,0:T(8,128)(2,1)S(1)}, bf16[1024,2048]{1,0:T(8,128)(2,1)}, u32[]{:S(2)}) copy-start(bf16[1024,2048]{1,0:T(8,128)(2,1)} %get-tuple-element.750) | copy-start | bytes 12582916 | tf_op jit(solution)/shard_map/while/body/eval_jaxpr/cond
  370.0 3.1 copy-start.3
  370.0 3.6 copy-start.1
  375.4 32.7 %collective-permute-start.2 = (bf16[1,32,2048]{2,1,0:T(8,128)(2,1)S(1)}, bf16[1,32,2048]{2,1,0:T(8,128)(2,1)S(1)}, u32[]{:S(2)}, u32[]{:S(2)}) collective-permute-start(bf16[1,32,2048]{2,1,0:T(8,128)(2,1)S(1)} %get-tuple-element.1160), channel_id=1, source_target_pairs={{16,0},{17,1},{18,2},{19,3},{20,4},{21,5},{22,6},{23,7},{24,8},{25... | collective-permute-start | bytes 393224 | tf_op jit(solution)/shard_map/while/body/eval_jaxpr/ppermute | solution.py:14
  376.7 31.4 %collective-permute-start.3 = (bf16[1,32,2048]{2,1,0:T(8,128)(2,1)S(1)}, bf16[1,32,2048]{2,1,0:T(8,128)(2,1)S(1)}, u32[]{:S(2)}, u32[]{:S(2)}) collective-permute-start(bf16[1,32,2048]{2,1,0:T(8,128)(2,1)S(1)} %get-tuple-element.1161), channel_id=1, source_target_pairs={{16,0},{17,1},{18,2},{19,3},{20,4},{21,5},{22,6},{23,7},{24,8},{25... | collective-permute-start | bytes 393224 | tf_op jit(solution)/shard_map/while/body/eval_jaxpr/ppermute | solution.py:14
  408.2 0.8 copy-start.5
  408.2 0.8 copy-start.6
Sparse Core Ops, SparseCore 0:
  10.2 53.2 all-gather.2
  65.6 49.0 all-gather.4
where the time goes:
time: 417 us; the launch traced here: 416 us
  blocking collectives  150 us (36%)
  waiting for transfers between devices  123 us (29%)
  matrix products  54.3 us (13%)
  starting transfers between devices  46.6 us (11%)
  other arithmetic  22.1 us (5%)
  between operations  14.2 us (3%)
    psum x5, blocking collectives, backward_tick(): gain_total = gain_total + lax.psum(gain_grad, 'fsdp')  150 us
    all_gather x1, waiting for transfers between devices, on_device(): lax.all_gather(output_weights, 'fsdp', axis=1, tiled=True)  53.6 us
    all_gather x1, waiting for transfers between devices, on_device(): lax.all_gather(query_weights, 'fsdp', axis=1, tiled=True)  51.2 us
    ppermute x20, starting transfers between devices, shifted(): return lax.ppermute(array, axis, pairs)  46.5 us
    dot_general x12, matrix products, attend_layer(): jnp.dot(normed_rows, query_weight, preferred_element_type=jnp.float32)  30.8 us
    dot_general x8, matrix products, attend_layer(): update = jnp.dot(mixed, output_weight, preferred_element_type=jnp.float32)  17.4 us
    ppermute x20, waiting for transfers between devices, shifted(): return lax.ppermute(array, axis, pairs)  17 us
  transfers between devices with their start and end apart: 22, of which 7 were waited for; matrix products, arithmetic and copies ran while one was open for 0% of the time, Pallas kernels for 0%

commit v1 on v0

--- a/solution.py
+++ b/solution.py
@@ -143,7 +143,7 @@
         send_side = jnp.where(is_decoder & (section_index != half_sections), memory_sum, zero_act)
         got_grad, got_memory_grad = shifted((send_main, send_side), "section", -1)
         grads_buf = place_slot(grads_buf, slot, input_grad, is_active)
-        gain_total = gain_total + lax.psum(gain_grad, "fsdp")
+        gain_total = gain_total + lax.all_gather(gain_grad, "fsdp").sum(axis=0)
         return (got_grad, got_memory_grad, grads_buf, gain_total)
 
     back_state = (zero_act, zero_act, zero_stack, jnp.zeros_like(gain_vector))

time: 417 us -> 361 us (0.87)
  blocking collectives: 150 us -> 93.1 us
    psum x5 -> x0, blocking collectives: 150 us -> none  [backward_tick(): gain_total = gain_total + lax.psum(gain_grad, 'fsdp')]
    all_gather x0 -> x5, blocking collectives: none -> 93.1 us  [backward_tick(): gain_total = gain_total + lax.all_gather(gain_grad, 'fsdp').sum(axis=0)]
  transfers between devices with their start and end apart: 22 -> 22, of which waited for: 7 -> 7; matrix products, arithmetic and copies ran while one was open for 0% -> 1% of each run, Pallas kernels for 0% -> 0%
where the time goes in v1:
time: 361 us; the launch traced here: 359 us
  waiting for transfers between devices  123 us (34%)
  blocking collectives  93.1 us (26%)
  matrix products  54.3 us (15%)
  starting transfers between devices  46.6 us (13%)
  other arithmetic  22.2 us (6%)
  between operations  14.2 us (4%)
    all_gather x5, blocking collectives, backward_tick(): gain_total = gain_total + lax.all_gather(gain_grad, 'fsdp').sum(axis=0)  93.1 us
    all_gather x1, waiting for transfers between devices, on_device(): lax.all_gather(output_weights, 'fsdp', axis=1, tiled=True)  53.6 us
    all_gather x1, waiting for transfers between devices, on_device(): lax.all_gather(query_weights, 'fsdp', axis=1, tiled=True)  51.2 us
    ppermute x20, starting transfers between devices, shifted(): return lax.ppermute(array, axis, pairs)  46.5 us
    dot_general x12, matrix products, attend_layer(): jnp.dot(normed_rows, query_weight, preferred_element_type=jnp.float32)  30.8 us
    dot_general x8, matrix products, attend_layer(): update = jnp.dot(mixed, output_weight, preferred_element_type=jnp.float32)  17.4 us
    ppermute x20, waiting for transfers between devices, shifted(): return lax.ppermute(array, axis, pairs)  17 us
  transfers between devices with their start and end apart: 22, of which 7 were waited for; matrix products, arithmetic and copies ran while one was open for 1% of the time, Pallas kernels for 0%

profile of v1, /device:TPU:0, one launch (start us, length us, event | category | flops | bytes accessed | tf_op | source)
XLA Modules:
  0.0 359.2 jit_solution(16348101874996884516)
XLA Ops:
  9.9 53.6 %all-gather.7.cloned.1.call-done = bf16[1,1024,2048]{2,1,0:T(8,128)(2,1)} async-done(((bf16[1,64,2048]{2,1,0:T(8,128)(2,1)}), bf16[1,1024,2048]{2,1,0:T(8,128)(2,1)}) %all-gather.7.cloned.1.call-update) | async-done | bytes 4194320 | tf_op jit(solution)/shard_map/all_gather | solution.py:65
  63.5 51.2 %all-gather.9.cloned.1.call-done = bf16[1,2048,1024]{2,1,0:T(8,128)(2,1)} async-done(((bf16[1,128,1024]{2,1,0:T(8,128)(2,1)}), bf16[1,2048,1024]{2,1,0:T(8,128)(2,1)}) %all-gather.9.cloned.1.call-update) | async-done | bytes 4194320 | tf_op jit(solution)/shard_map/all_gather | solution.py:64
  114.9 89.8 %while.42 = (s32[]{:T(128)}, bf16[1,32,2048]{2,1,0:T(8,128)(2,1)S(1)}, bf16[1,32,2048]{2,1,0:T(8,128)(2,1)S(1)}, bf16[4,1,32,2048]{3,2,1,0:T(8,128)(2,1)S(1)}, b...) while((s32[]{:T(128)}, ...), condition=%wide.region_6.7_spmd, body=%wide.region_0.6_spmd.sunk | while | flops 274366848 | bytes 14173985 | solution.py:113
  114.9 1.0 bitcast_dynamic-update-slice_fusion.6
  116.0 8.3 %conditional.5 = (bf16[1,32,2048]{2,1,0:T(8,128)(2,1)S(1)}) conditional(s32[]{:T(128)} %convert_element_type.398, () %tuple.122, (bf16[1,32,2048]{2,1,0:T(8,128)(2,1)S(1)}, pred[1,32,2048]{2,1,0:T(8,128)(4,1)S(1)}, bf16[1,32,2048]{2,1,0:T(8,128)(2,1)S(1)}, f32[1,2048]{1,0:T(1,128)}, bf16[2048,1024]{1,0:T(8,128)(2,1)}, ...), branch_computations={%region_1.1_spmd, %region_2.5_spmd} | conditional | flops 273973632 | bytes 10700172 | solution.py:103
  117.0 3.1 fusion.5
  121.2 3.0 fusion.1
  124.3 1.3 collective-permute-start
  125.6 1.3 collective-permute-start.1
  127.0 4.8 %collective-permute-done.1 = bf16[1,32,2048]{2,1,0:T(8,128)(2,1)S(1)} collective-permute-done((bf16[1,32,2048]{2,1,0:T(8,128)(2,1)S(1)}, bf16[1,32,2048]{2,1,0:T(8,128)(2,1)S(1)}, u32[]{:S(2)}, u32[]{:S(2)}) %collective-permute-start.1) | collective-permute-done | bytes 131104 | tf_op jit(solution)/shard_map/while/body/eval_jaxpr/ppermute | solution.py:14
  132.9 8.3 %conditional.5 = (bf16[1,32,2048]{2,1,0:T(8,128)(2,1)S(1)}) conditional(s32[]{:T(128)} %convert_element_type.398, () %tuple.122, (bf16[1,32,2048]{2,1,0:T(8,128)(2,1)S(1)}, pred[1,32,2048]{2,1,0:T(8,128)(4,1)S(1)}, bf16[1,32,2048]{2,1,0:T(8,128)(2,1)S(1)}, f32[1,2048]{1,0:T(1,128)}, bf16[2048,1024]{1,0:T(8,128)(2,1)}, ...), branch_computations={%region_1.1_spmd, %region_2.5_spmd} | conditional | flops 273973632 | bytes 10700172 | solution.py:103
  134.0 3.1 fusion.5
  138.2 3.0 fusion.1
  141.2 4.4 %collective-permute-start = (bf16[1,32,2048]{2,1,0:T(8,128)(2,1)S(1)}, bf16[1,32,2048]{2,1,0:T(8,128)(2,1)S(1)}, u32[]{:S(2)}, u32[]{:S(2)}) collective-permute-start(bf16[1,32,2048]{2,1,0:T(8,128)(2,1)S(1)} %get-tuple-element.1319), channel_id=1, source_target_pairs={{0,16},{1,17},{2,18},{3,19},{4,20},{5,21},{6,22},{7,23},{8,24},{9,... | collective-permute-start | bytes 393224 | tf_op jit(solution)/shard_map/while/body/eval_jaxpr/ppermute | solution.py:14
  145.6 1.3 collective-permute-start.1
  147.0 4.0 %collective-permute-done.1 = bf16[1,32,2048]{2,1,0:T(8,128)(2,1)S(1)} collective-permute-done((bf16[1,32,2048]{2,1,0:T(8,128)(2,1)S(1)}, bf16[1,32,2048]{2,1,0:T(8,128)(2,1)S(1)}, u32[]{:S(2)}, u32[]{:S(2)}) %collective-permute-start.1) | collective-permute-done | bytes 131104 | tf_op jit(solution)/shard_map/while/body/eval_jaxpr/ppermute | solution.py:14
  151.1 1.0 bitcast_dynamic-update-slice_fusion.6
  152.1 8.3 %conditional.5 = (bf16[1,32,2048]{2,1,0:T(8,128)(2,1)S(1)}) conditional(s32[]{:T(128)} %convert_element_type.398, () %tuple.122, (bf16[1,32,2048]{2,1,0:T(8,128)(2,1)S(1)}, pred[1,32,2048]{2,1,0:T(8,128)(4,1)S(1)}, bf16[1,32,2048]{2,1,0:T(8,128)(2,1)S(1)}, f32[1,2048]{1,0:T(1,128)}, bf16[2048,1024]{1,0:T(8,128)(2,1)}, ...), branch_computations={%region_1.1_spmd, %region_2.5_spmd} | conditional | flops 273973632 | bytes 10700172 | solution.py:103
  153.2 3.1 fusion.5
  157.4 3.0 fusion.1
  160.4 4.4 %collective-permute-start = (bf16[1,32,2048]{2,1,0:T(8,128)(2,1)S(1)}, bf16[1,32,2048]{2,1,0:T(8,128)(2,1)S(1)}, u32[]{:S(2)}, u32[]{:S(2)}) collective-permute-start(bf16[1,32,2048]{2,1,0:T(8,128)(2,1)S(1)} %get-tuple-element.1319), channel_id=1, source_target_pairs={{0,16},{1,17},{2,18},{3,19},{4,20},{5,21},{6,22},{7,23},{8,24},{9,... | collective-permute-start | bytes 393224 | tf_op jit(solution)/shard_map/while/body/eval_jaxpr/ppermute | solution.py:14
  164.8 1.3 collective-permute-start.1
  166.2 3.2 collective-permute-done.1
  170.5 8.3 %conditional.5 = (bf16[1,32,2048]{2,1,0:T(8,128)(2,1)S(1)}) conditional(s32[]{:T(128)} %convert_element_type.398, () %tuple.122, (bf16[1,32,2048]{2,1,0:T(8,128)(2,1)S(1)}, pred[1,32,2048]{2,1,0:T(8,128)(4,1)S(1)}, bf16[1,32,2048]{2,1,0:T(8,128)(2,1)S(1)}, f32[1,2048]{1,0:T(1,128)}, bf16[2048,1024]{1,0:T(8,128)(2,1)}, ...), branch_computations={%region_1.1_spmd, %region_2.5_spmd} | conditional | flops 273973632 | bytes 10700172 | solution.py:103
  171.5 3.1 fusion.5
  175.7 3.0 fusion.1
  178.8 4.4 %collective-permute-start = (bf16[1,32,2048]{2,1,0:T(8,128)(2,1)S(1)}, bf16[1,32,2048]{2,1,0:T(8,128)(2,1)S(1)}, u32[]{:S(2)}, u32[]{:S(2)}) collective-permute-start(bf16[1,32,2048]{2,1,0:T(8,128)(2,1)S(1)} %get-tuple-element.1319), channel_id=1, source_target_pairs={{0,16},{1,17},{2,18},{3,19},{4,20},{5,21},{6,22},{7,23},{8,24},{9,... | collective-permute-start | bytes 393224 | tf_op jit(solution)/shard_map/while/body/eval_jaxpr/ppermute | solution.py:14
  183.2 1.3 collective-permute-start.1
  184.6 2.5 collective-permute-done.1
  188.2 12.6 %collective-permute-start = (bf16[1,32,2048]{2,1,0:T(8,128)(2,1)S(1)}, bf16[1,32,2048]{2,1,0:T(8,128)(2,1)S(1)}, u32[]{:S(2)}, u32[]{:S(2)}) collective-permute-start(bf16[1,32,2048]{2,1,0:T(8,128)(2,1)S(1)} %get-tuple-element.1319), channel_id=1, source_target_pairs={{0,16},{1,17},{2,18},{3,19},{4,20},{5,21},{6,22},{7,23},{8,24},{9,... | collective-permute-start | bytes 393224 | tf_op jit(solution)/shard_map/while/body/eval_jaxpr/ppermute | solution.py:14
  200.8 1.3 collective-permute-start.1
  202.2 2.5 collective-permute-done.1
  204.8 146.7 %while.43 = (s32[]{:T(128)}, bf16[1,32,2048]{2,1,0:T(8,128)(2,1)S(1)}, bf16[1,32,2048]{2,1,0:T(8,128)(2,1)S(1)}, bf16[4,1,32,2048]{3,2,1,0:T(8,128)(2,1)S(1)}, f...) while((s32[]{:T(128)}, ...), condition=%wide.region_19.20_spmd.clone, body=%wide.region_7.19_spmd.clone.sunk | while | flops 417645216 | bytes 54706752 | solution.py:150
  205.0 1.3 collective-permute-start.2
  206.3 1.3 collective-permute-start.3
  207.6 19.3 %all-gather.3 = f32[32768]{0:T(1024)S(1)} all-gather(f32[2048]{0:T(1024)S(1)} %get-tuple-element.1192), channel_id=2, replica_groups=mesh['section'=2,'fsdp'=16] {'fsdp'}, dimensions={0}, use_global_device_ids=true | all-gather | bytes 139264 | tf_op jit(solution)/shard_map/while/body/eval_jaxpr/all_gather | solution.py:146
  227.1 9.8 %conditional.6 = (bf16[1,32,2048]{2,1,0:T(8,128)(2,1)S(1)}, bf16[1,32,2048]{2,1,0:T(8,128)(2,1)S(1)}, f32[2048]{0:T(1024)S(1)}) conditional(s32[]{:T(128)} %convert_element_type.399, () %tuple.126, (bf16[4,1,32,2048]{3,2,1,0:T(8,128)(2,1)S(1)}, s32[]{:T(128)}, pred[1,32,2048]{2,1,0:T(32,128)(4,1)S(1)}, bf16[1,32,2048]{2,1,0:T(8,128)(2,1)S(1)}, ...), branch_computations={%region_8.8_spmd, %region_9.17_spmd} | conditional | flops 417282720 | bytes 51716228 | solution.py:140
  228.3 3.1 fusion.38
  232.5 1.3 fusion.37
  235.1 1.5 fusion.50
  236.9 1.3 collective-permute-start.2
  238.2 1.3 collective-permute-start.3
  239.6 17.8 %all-gather.3 = f32[32768]{0:T(1024)S(1)} all-gather(f32[2048]{0:T(1024)S(1)} %get-tuple-element.1192), channel_id=2, replica_groups=mesh['section'=2,'fsdp'=16] {'fsdp'}, dimensions={0}, use_global_device_ids=true | all-gather | bytes 139264 | tf_op jit(solution)/shard_map/while/body/eval_jaxpr/all_gather | solution.py:146
  257.6 9.8 %conditional.6 = (bf16[1,32,2048]{2,1,0:T(8,128)(2,1)S(1)}, bf16[1,32,2048]{2,1,0:T(8,128)(2,1)S(1)}, f32[2048]{0:T(1024)S(1)}) conditional(s32[]{:T(128)} %convert_element_type.399, () %tuple.126, (bf16[4,1,32,2048]{3,2,1,0:T(8,128)(2,1)S(1)}, s32[]{:T(128)}, pred[1,32,2048]{2,1,0:T(32,128)(4,1)S(1)}, bf16[1,32,2048]{2,1,0:T(8,128)(2,1)S(1)}, ...), branch_computations={%region_8.8_spmd, %region_9.17_spmd} | conditional | flops 417282720 | bytes 51716228 | solution.py:140
  258.8 3.1 fusion.38
  263.0 1.3 fusion.37
  265.5 1.5 fusion.50
  267.4 1.3 collective-permute-start.2
  268.7 1.3 collective-permute-start.3
  270.1 19.1 %all-gather.3 = f32[32768]{0:T(1024)S(1)} all-gather(f32[2048]{0:T(1024)S(1)} %get-tuple-element.1192), channel_id=2, replica_groups=mesh['section'=2,'fsdp'=16] {'fsdp'}, dimensions={0}, use_global_device_ids=true | all-gather | bytes 139264 | tf_op jit(solution)/shard_map/while/body/eval_jaxpr/all_gather | solution.py:146
  289.4 9.8 %conditional.6 = (bf16[1,32,2048]{2,1,0:T(8,128)(2,1)S(1)}, bf16[1,32,2048]{2,1,0:T(8,128)(2,1)S(1)}, f32[2048]{0:T(1024)S(1)}) conditional(s32[]{:T(128)} %convert_element_type.399, () %tuple.126, (bf16[4,1,32,2048]{3,2,1,0:T(8,128)(2,1)S(1)}, s32[]{:T(128)}, pred[1,32,2048]{2,1,0:T(32,128)(4,1)S(1)}, bf16[1,32,2048]{2,1,0:T(8,128)(2,1)S(1)}, ...), branch_computations={%region_8.8_spmd, %region_9.17_spmd} | conditional | flops 417282720 | bytes 51716228 | solution.py:140
  290.6 3.1 fusion.38
  294.8 1.3 fusion.37
  297.3 1.5 fusion.50
  299.2 1.3 collective-permute-start.2
  300.5 1.3 collective-permute-start.3
  301.9 17.8 %all-gather.3 = f32[32768]{0:T(1024)S(1)} all-gather(f32[2048]{0:T(1024)S(1)} %get-tuple-element.1192), channel_id=2, replica_groups=mesh['section'=2,'fsdp'=16] {'fsdp'}, dimensions={0}, use_global_device_ids=true | all-gather | bytes 139264 | tf_op jit(solution)/shard_map/while/body/eval_jaxpr/all_gather | solution.py:146
  319.8 9.8 %conditional.6 = (bf16[1,32,2048]{2,1,0:T(8,128)(2,1)S(1)}, bf16[1,32,2048]{2,1,0:T(8,128)(2,1)S(1)}, f32[2048]{0:T(1024)S(1)}) conditional(s32[]{:T(128)} %convert_element_type.399, () %tuple.126, (bf16[4,1,32,2048]{3,2,1,0:T(8,128)(2,1)S(1)}, s32[]{:T(128)}, pred[1,32,2048]{2,1,0:T(32,128)(4,1)S(1)}, bf16[1,32,2048]{2,1,0:T(8,128)(2,1)S(1)}, ...), branch_computations={%region_8.8_spmd, %region_9.17_spmd} | conditional | flops 417282720 | bytes 51716228 | solution.py:140
  321.0 3.1 fusion.38
  325.2 1.3 fusion.37
  327.8 1.5 fusion.50
  329.7 1.3 collective-permute-start.2
  331.0 1.3 collective-permute-start.3
  332.3 19.1 %all-gather.3 = f32[32768]{0:T(1024)S(1)} all-gather(f32[2048]{0:T(1024)S(1)} %get-tuple-element.1192), channel_id=2, replica_groups=mesh['section'=2,'fsdp'=16] {'fsdp'}, dimensions={0}, use_global_device_ids=true | all-gather | bytes 139264 | tf_op jit(solution)/shard_map/while/body/eval_jaxpr/all_gather | solution.py:146
  (272 shorter events, 31.2 us)
Async XLA Ops:
  7.2 2.4 copy-start
  7.2 56.3 %all-gather.7.cloned.1.call-start = ((), (), s32[]{:S(2)}) async-start(), calls=%async_computation | async-start | bytes 4456448 | tf_op jit(solution)/shard_map/all_gather | solution.py:65
  7.9 106.8 %all-gather.9.cloned.1.call-start = ((), (), s32[]{:S(2)}) async-start(), calls=%async_computation.1 | async-start | bytes 4456448 | tf_op jit(solution)/shard_map/all_gather | solution.py:64
  114.9 89.9 %copy-start.4 = (bf16[4,1,32,2048]{3,2,1,0:T(8,128)(2,1)S(1)}, bf16[4,1,32,2048]{3,2,1,0:T(8,128)(2,1)}, u32[]{:S(2)}) copy-start(bf16[4,1,32,2048]{3,2,1,0:T(8,128)(2,1)} %param.23) | copy-start | bytes 1572868
  124.3 7.6 %collective-permute-start = (bf16[1,32,2048]{2,1,0:T(8,128)(2,1)S(1)}, bf16[1,32,2048]{2,1,0:T(8,128)(2,1)S(1)}, u32[]{:S(2)}, u32[]{:S(2)}) collective-permute-start(bf16[1,32,2048]{2,1,0:T(8,128)(2,1)S(1)} %get-tuple-element.1319), channel_id=1, source_target_pairs={{0,16},{1,17},{2,18},{3,19},{4,20},{5,21},{6,22},{7,23},{8,24},{9,... | collective-permute-start | bytes 393224 | tf_op jit(solution)/shard_map/while/body/eval_jaxpr/ppermute | solution.py:14
  125.6 6.2 %collective-permute-start.1 = (bf16[1,32,2048]{2,1,0:T(8,128)(2,1)S(1)}, bf16[1,32,2048]{2,1,0:T(8,128)(2,1)S(1)}, u32[]{:S(2)}, u32[]{:S(2)}) collective-permute-start(bf16[1,32,2048]{2,1,0:T(8,128)(2,1)S(1)} %select_select_fusion.2), channel_id=1, source_target_pairs={{0,16},{1,17},{2,18},{3,19},{4,20},{5,21},{6,22},{7,23},{8,24},{9,... | collective-permute-start | bytes 393224 | tf_op jit(solution)/shard_map/while/body/eval_jaxpr/ppermute | solution.py:14
  141.2 9.9 %collective-permute-start = (bf16[1,32,2048]{2,1,0:T(8,128)(2,1)S(1)}, bf16[1,32,2048]{2,1,0:T(8,128)(2,1)S(1)}, u32[]{:S(2)}, u32[]{:S(2)}) collective-permute-start(bf16[1,32,2048]{2,1,0:T(8,128)(2,1)S(1)} %get-tuple-element.1319), channel_id=1, source_target_pairs={{0,16},{1,17},{2,18},{3,19},{4,20},{5,21},{6,22},{7,23},{8,24},{9,... | collective-permute-start | bytes 393224 | tf_op jit(solution)/shard_map/while/body/eval_jaxpr/ppermute | solution.py:14
  145.6 5.4 %collective-permute-start.1 = (bf16[1,32,2048]{2,1,0:T(8,128)(2,1)S(1)}, bf16[1,32,2048]{2,1,0:T(8,128)(2,1)S(1)}, u32[]{:S(2)}, u32[]{:S(2)}) collective-permute-start(bf16[1,32,2048]{2,1,0:T(8,128)(2,1)S(1)} %select_select_fusion.2), channel_id=1, source_target_pairs={{0,16},{1,17},{2,18},{3,19},{4,20},{5,21},{6,22},{7,23},{8,24},{9,... | collective-permute-start | bytes 393224 | tf_op jit(solution)/shard_map/while/body/eval_jaxpr/ppermute | solution.py:14
  160.4 9.0 %collective-permute-start = (bf16[1,32,2048]{2,1,0:T(8,128)(2,1)S(1)}, bf16[1,32,2048]{2,1,0:T(8,128)(2,1)S(1)}, u32[]{:S(2)}, u32[]{:S(2)}) collective-permute-start(bf16[1,32,2048]{2,1,0:T(8,128)(2,1)S(1)} %get-tuple-element.1319), channel_id=1, source_target_pairs={{0,16},{1,17},{2,18},{3,19},{4,20},{5,21},{6,22},{7,23},{8,24},{9,... | collective-permute-start | bytes 393224 | tf_op jit(solution)/shard_map/while/body/eval_jaxpr/ppermute | solution.py:14
  164.8 4.5 %collective-permute-start.1 = (bf16[1,32,2048]{2,1,0:T(8,128)(2,1)S(1)}, bf16[1,32,2048]{2,1,0:T(8,128)(2,1)S(1)}, u32[]{:S(2)}, u32[]{:S(2)}) collective-permute-start(bf16[1,32,2048]{2,1,0:T(8,128)(2,1)S(1)} %select_select_fusion.2), channel_id=1, source_target_pairs={{0,16},{1,17},{2,18},{3,19},{4,20},{5,21},{6,22},{7,23},{8,24},{9,... | collective-permute-start | bytes 393224 | tf_op jit(solution)/shard_map/while/body/eval_jaxpr/ppermute | solution.py:14
  178.8 8.3 %collective-permute-start = (bf16[1,32,2048]{2,1,0:T(8,128)(2,1)S(1)}, bf16[1,32,2048]{2,1,0:T(8,128)(2,1)S(1)}, u32[]{:S(2)}, u32[]{:S(2)}) collective-permute-start(bf16[1,32,2048]{2,1,0:T(8,128)(2,1)S(1)} %get-tuple-element.1319), channel_id=1, source_target_pairs={{0,16},{1,17},{2,18},{3,19},{4,20},{5,21},{6,22},{7,23},{8,24},{9,... | collective-permute-start | bytes 393224 | tf_op jit(solution)/shard_map/while/body/eval_jaxpr/ppermute | solution.py:14
  183.2 3.8 %collective-permute-start.1 = (bf16[1,32,2048]{2,1,0:T(8,128)(2,1)S(1)}, bf16[1,32,2048]{2,1,0:T(8,128)(2,1)S(1)}, u32[]{:S(2)}, u32[]{:S(2)}) collective-permute-start(bf16[1,32,2048]{2,1,0:T(8,128)(2,1)S(1)} %select_select_fusion.2), channel_id=1, source_target_pairs={{0,16},{1,17},{2,18},{3,19},{4,20},{5,21},{6,22},{7,23},{8,24},{9,... | collective-permute-start | bytes 393224 | tf_op jit(solution)/shard_map/while/body/eval_jaxpr/ppermute | solution.py:14
  188.2 16.5 %collective-permute-start = (bf16[1,32,2048]{2,1,0:T(8,128)(2,1)S(1)}, bf16[1,32,2048]{2,1,0:T(8,128)(2,1)S(1)}, u32[]{:S(2)}, u32[]{:S(2)}) collective-permute-start(bf16[1,32,2048]{2,1,0:T(8,128)(2,1)S(1)} %get-tuple-element.1319), channel_id=1, source_target_pairs={{0,16},{1,17},{2,18},{3,19},{4,20},{5,21},{6,22},{7,23},{8,24},{9,... | collective-permute-start | bytes 393224 | tf_op jit(solution)/shard_map/while/body/eval_jaxpr/ppermute | solution.py:14
  200.8 3.8 %collective-permute-start.1 = (bf16[1,32,2048]{2,1,0:T(8,128)(2,1)S(1)}, bf16[1,32,2048]{2,1,0:T(8,128)(2,1)S(1)}, u32[]{:S(2)}, u32[]{:S(2)}) collective-permute-start(bf16[1,32,2048]{2,1,0:T(8,128)(2,1)S(1)} %select_select_fusion.2), channel_id=1, source_target_pairs={{0,16},{1,17},{2,18},{3,19},{4,20},{5,21},{6,22},{7,23},{8,24},{9,... | collective-permute-start | bytes 393224 | tf_op jit(solution)/shard_map/while/body/eval_jaxpr/ppermute | solution.py:14
  205.0 22.1 %collective-permute-start.2 = (bf16[1,32,2048]{2,1,0:T(8,128)(2,1)S(1)}, bf16[1,32,2048]{2,1,0:T(8,128)(2,1)S(1)}, u32[]{:S(2)}, u32[]{:S(2)}) collective-permute-start(bf16[1,32,2048]{2,1,0:T(8,128)(2,1)S(1)} %get-tuple-element.1190), channel_id=1, source_target_pairs={{16,0},{17,1},{18,2},{19,3},{20,4},{21,5},{22,6},{23,7},{24,8},{25... | collective-permute-start | bytes 393224 | tf_op jit(solution)/shard_map/while/body/eval_jaxpr/ppermute | solution.py:14
  206.3 20.8 %collective-permute-start.3 = (bf16[1,32,2048]{2,1,0:T(8,128)(2,1)S(1)}, bf16[1,32,2048]{2,1,0:T(8,128)(2,1)S(1)}, u32[]{:S(2)}, u32[]{:S(2)}) collective-permute-start(bf16[1,32,2048]{2,1,0:T(8,128)(2,1)S(1)} %get-tuple-element.1191), channel_id=1, source_target_pairs={{16,0},{17,1},{18,2},{19,3},{20,4},{21,5},{22,6},{23,7},{24,8},{25... | collective-permute-start | bytes 393224 | tf_op jit(solution)/shard_map/while/body/eval_jaxpr/ppermute | solution.py:14
  227.1 5.4 %copy-start.2 = (bf16[1024,2048]{1,0:T(8,128)(2,1)S(1)}, bf16[1024,2048]{1,0:T(8,128)(2,1)}, u32[]{:S(2)}) copy-start(bf16[1024,2048]{1,0:T(8,128)(2,1)} %get-tuple-element.750) | copy-start | bytes 12582916 | tf_op jit(solution)/shard_map/while/body/eval_jaxpr/cond
  231.5 3.1 copy-start.3
  231.5 3.6 copy-start.1
  236.9 20.5 %collective-permute-start.2 = (bf16[1,32,2048]{2,1,0:T(8,128)(2,1)S(1)}, bf16[1,32,2048]{2,1,0:T(8,128)(2,1)S(1)}, u32[]{:S(2)}, u32[]{:S(2)}) collective-permute-start(bf16[1,32,2048]{2,1,0:T(8,128)(2,1)S(1)} %get-tuple-element.1190), channel_id=1, source_target_pairs={{16,0},{17,1},{18,2},{19,3},{20,4},{21,5},{22,6},{23,7},{24,8},{25... | collective-permute-start | bytes 393224 | tf_op jit(solution)/shard_map/while/body/eval_jaxpr/ppermute | solution.py:14
  238.2 19.3 %collective-permute-start.3 = (bf16[1,32,2048]{2,1,0:T(8,128)(2,1)S(1)}, bf16[1,32,2048]{2,1,0:T(8,128)(2,1)S(1)}, u32[]{:S(2)}, u32[]{:S(2)}) collective-permute-start(bf16[1,32,2048]{2,1,0:T(8,128)(2,1)S(1)} %get-tuple-element.1191), channel_id=1, source_target_pairs={{16,0},{17,1},{18,2},{19,3},{20,4},{21,5},{22,6},{23,7},{24,8},{25... | collective-permute-start | bytes 393224 | tf_op jit(solution)/shard_map/while/body/eval_jaxpr/ppermute | solution.py:14
  257.6 5.4 %copy-start.2 = (bf16[1024,2048]{1,0:T(8,128)(2,1)S(1)}, bf16[1024,2048]{1,0:T(8,128)(2,1)}, u32[]{:S(2)}) copy-start(bf16[1024,2048]{1,0:T(8,128)(2,1)} %get-tuple-element.750) | copy-start | bytes 12582916 | tf_op jit(solution)/shard_map/while/body/eval_jaxpr/cond
  261.9 3.1 copy-start.3
  261.9 3.6 copy-start.1
  267.4 21.9 %collective-permute-start.2 = (bf16[1,32,2048]{2,1,0:T(8,128)(2,1)S(1)}, bf16[1,32,2048]{2,1,0:T(8,128)(2,1)S(1)}, u32[]{:S(2)}, u32[]{:S(2)}) collective-permute-start(bf16[1,32,2048]{2,1,0:T(8,128)(2,1)S(1)} %get-tuple-element.1190), channel_id=1, source_target_pairs={{16,0},{17,1},{18,2},{19,3},{20,4},{21,5},{22,6},{23,7},{24,8},{25... | collective-permute-start | bytes 393224 | tf_op jit(solution)/shard_map/while/body/eval_jaxpr/ppermute | solution.py:14
  268.7 20.6 %collective-permute-start.3 = (bf16[1,32,2048]{2,1,0:T(8,128)(2,1)S(1)}, bf16[1,32,2048]{2,1,0:T(8,128)(2,1)S(1)}, u32[]{:S(2)}, u32[]{:S(2)}) collective-permute-start(bf16[1,32,2048]{2,1,0:T(8,128)(2,1)S(1)} %get-tuple-element.1191), channel_id=1, source_target_pairs={{16,0},{17,1},{18,2},{19,3},{20,4},{21,5},{22,6},{23,7},{24,8},{25... | collective-permute-start | bytes 393224 | tf_op jit(solution)/shard_map/while/body/eval_jaxpr/ppermute | solution.py:14
  289.4 5.4 %copy-start.2 = (bf16[1024,2048]{1,0:T(8,128)(2,1)S(1)}, bf16[1024,2048]{1,0:T(8,128)(2,1)}, u32[]{:S(2)}) copy-start(bf16[1024,2048]{1,0:T(8,128)(2,1)} %get-tuple-element.750) | copy-start | bytes 12582916 | tf_op jit(solution)/shard_map/while/body/eval_jaxpr/cond
  293.7 3.1 copy-start.3
  293.7 3.6 copy-start.1
  299.2 20.5 %collective-permute-start.2 = (bf16[1,32,2048]{2,1,0:T(8,128)(2,1)S(1)}, bf16[1,32,2048]{2,1,0:T(8,128)(2,1)S(1)}, u32[]{:S(2)}, u32[]{:S(2)}) collective-permute-start(bf16[1,32,2048]{2,1,0:T(8,128)(2,1)S(1)} %get-tuple-element.1190), channel_id=1, source_target_pairs={{16,0},{17,1},{18,2},{19,3},{20,4},{21,5},{22,6},{23,7},{24,8},{25... | collective-permute-start | bytes 393224 | tf_op jit(solution)/shard_map/while/body/eval_jaxpr/ppermute | solution.py:14
  300.5 19.3 %collective-permute-start.3 = (bf16[1,32,2048]{2,1,0:T(8,128)(2,1)S(1)}, bf16[1,32,2048]{2,1,0:T(8,128)(2,1)S(1)}, u32[]{:S(2)}, u32[]{:S(2)}) collective-permute-start(bf16[1,32,2048]{2,1,0:T(8,128)(2,1)S(1)} %get-tuple-element.1191), channel_id=1, source_target_pairs={{16,0},{17,1},{18,2},{19,3},{20,4},{21,5},{22,6},{23,7},{24,8},{25... | collective-permute-start | bytes 393224 | tf_op jit(solution)/shard_map/while/body/eval_jaxpr/ppermute | solution.py:14
  319.8 5.4 %copy-start.2 = (bf16[1024,2048]{1,0:T(8,128)(2,1)S(1)}, bf16[1024,2048]{1,0:T(8,128)(2,1)}, u32[]{:S(2)}) copy-start(bf16[1024,2048]{1,0:T(8,128)(2,1)} %get-tuple-element.750) | copy-start | bytes 12582916 | tf_op jit(solution)/shard_map/while/body/eval_jaxpr/cond
  324.2 3.1 copy-start.3
  324.2 3.6 copy-start.1
  329.7 21.9 %collective-permute-start.2 = (bf16[1,32,2048]{2,1,0:T(8,128)(2,1)S(1)}, bf16[1,32,2048]{2,1,0:T(8,128)(2,1)S(1)}, u32[]{:S(2)}, u32[]{:S(2)}) collective-permute-start(bf16[1,32,2048]{2,1,0:T(8,128)(2,1)S(1)} %get-tuple-element.1190), channel_id=1, source_target_pairs={{16,0},{17,1},{18,2},{19,3},{20,4},{21,5},{22,6},{23,7},{24,8},{25... | collective-permute-start | bytes 393224 | tf_op jit(solution)/shard_map/while/body/eval_jaxpr/ppermute | solution.py:14
  331.0 20.6 %collective-permute-start.3 = (bf16[1,32,2048]{2,1,0:T(8,128)(2,1)S(1)}, bf16[1,32,2048]{2,1,0:T(8,128)(2,1)S(1)}, u32[]{:S(2)}, u32[]{:S(2)}) collective-permute-start(bf16[1,32,2048]{2,1,0:T(8,128)(2,1)S(1)} %get-tuple-element.1191), channel_id=1, source_target_pairs={{16,0},{17,1},{18,2},{19,3},{20,4},{21,5},{22,6},{23,7},{24,8},{25... | collective-permute-start | bytes 393224 | tf_op jit(solution)/shard_map/while/body/eval_jaxpr/ppermute | solution.py:14
  351.6 0.8 copy-start.5
  351.6 0.8 copy-start.6
Sparse Core Ops, SparseCore 0:
  10.2 53.2 all-gather.6
  65.6 49.0 all-gather.8
